TPU v7x, 128 devices: a whole 4x4x4 slice. The times are simulated.
128 devices in a mesh: shard: 8 (over y, core), tensor: 4 (over z), section: 4 (over x).
Axes of the slice: x: 4, y: 4, z: 4, core: 2. Of those that a mesh axis runs over, the one named last changes fastest.
Arguments:
- activations: bfloat16 [4, 16384, 2048], P('section', 'shard'), may hold values from -500 to 500, as said below
- out_grad: bfloat16 [4, 16384, 8192], P('section', 'shard', 'tensor'), may hold values from -30 to 30, as said below
- basis: float32 [4, 2048, 256], P('section', 'shard'), may hold values from -0.125 to 0.125
- first_moment: float32 [4, 256, 8192], P('section', 'shard', 'tensor'), may hold values from -6 to 6
- second_moment: float32 [4, 256, 8192], P('section', 'shard', 'tensor'), may hold values from 0.5 to 2
- gain_partial: float32 [4, 8, 2048], P('section', 'shard'), may hold values from -4096 to 4096
- gain_first: float32 [4, 2048], P('section', 'shard'), may hold values from -6 to 6
- gain_second: float32 [4, 2048], P('section', 'shard'), may hold values from 0.5 to 2
Outputs:
- update: float32 [4, 2048, 8192], P('section', 'shard', 'tensor')
- first_out: float32 [4, 256, 8192], P('section', 'shard', 'tensor')
- second_out: float32 [4, 256, 8192], P('section', 'shard', 'tensor')
- new_basis: float32 [4, 2048, 256], P('section', ('shard', 'tensor'))
- gain_step: float32 [4, 2048], P('section', 'shard')
- gain_first_out: float32 [4, 2048], P('section', 'shard')
- gain_second_out: float32 [4, 2048], P('section', 'shard')
Inputs may be any that keep to these rules, and one draw needn't show every extreme that they name: Real-valued activations whose column scales differ from column to column. `out_grad`: Real-valued gradients whose column scales differ from column to column.
All inputs are finite; a program needn't handle non-finite values.
Results may differ from a plain program's by a relative error of at most 0.0003.
Values sent between devices are 32-bit elements; how exact they have to be, the bound alone decides.
No kernel may reach another device: no remote copies, remote signals or barrier semaphores. Data moves between devices by JAX's collectives and lax.ppermute only.
A program may use at most 128 MiB of HBM per device.

v0:
```python
import jax
import jax.numpy as jnp
from jax import lax
from jax.sharding import PartitionSpec as P

D = 2048
FF = 8192
NS_STEPS = 5
STEP = 8
exact_mode = lax.Precision.HIGHEST
beta_one = 0.9
beta_two = 0.999
adam_eps = 1e-08
clip_eps = 1e-06
ns_eps = 1e-07
coef_first = 3.4445
coef_second = -4.775
coef_third = 2.0315


def adam_direction(clipped, first_old, second_old):
    first_new = beta_one * first_old + (1.0 - beta_one) * clipped
    second_new = beta_two * second_old + (1.0 - beta_two) * clipped * clipped
    direction = (
        first_new
        / (1.0 - beta_one**STEP)
        / (jnp.sqrt(second_new / (1.0 - beta_two**STEP)) + adam_eps)
    )
    return (first_new, second_new, direction)


def ns_update(current, gram):
    mixer = coef_second * gram + coef_third * jnp.dot(gram, gram, precision=exact_mode)
    return coef_first * current + jnp.dot(current, mixer, precision=exact_mode)


def gram_of(block):
    local_gram = jnp.dot(block.T, block, precision=exact_mode)
    return lax.psum(local_gram, ("shard", "tensor"))


def shards(
    activations, out_grad, basis, first_moment, second_moment, gain_partial, gain_first, gain_second
):
    tensors = lax.axis_size("tensor")
    shard_pos = lax.axis_index("shard")
    layer_count = activations.shape[0]
    rows_here = basis.shape[1]
    rank_rows = first_moment.shape[1]
    cols_here = out_grad.shape[2]
    layer_index = 0
    tokens_in = activations[layer_index]
    grads_out = out_grad[layer_index]
    basis_here = basis[layer_index]

    def row_term(start, count, tokens_in=tokens_in, grads_out=grads_out):
        return lax.dot_general(
            tokens_in, grads_out, (((0,), (0,)), ((), ())), preferred_element_type=jnp.float32
        )

    grad_block = lax.psum_scatter(
        row_term(jnp.int32(0), lax.axis_size("shard") * rows_here),
        "shard",
        scatter_dimension=0,
        tiled=True,
    )
    part_proj = jnp.dot(basis_here.T, grad_block, precision=exact_mode)
    proj_full, gain_total = lax.psum((part_proj, gain_partial[layer_index, 0]), "shard")
    proj_rows = lax.dynamic_slice_in_dim(proj_full, shard_pos * rank_rows, rank_rows, 0)
    square_sum = jnp.sum(grad_block * grad_block)

    def refresh_term(start, count, grad_block=grad_block, proj_full=proj_full):
        return lax.dot_general(
            grad_block, proj_full, (((1,), (1,)), ((), ())), precision=exact_mode
        )

    refreshed = lax.psum_scatter(
        refresh_term(jnp.int32(0), lax.axis_size("tensor") * (rows_here // tensors)),
        "tensor",
        scatter_dimension=0,
        tiled=True,
    )
    kept_list = [basis_here]
    gain_own = lax.dynamic_slice_in_dim(gain_total, shard_pos * rows_here, rows_here, 0)
    square_sum = square_sum + jnp.sum(gain_own * gain_own) / float(tensors)
    proj_list = [proj_rows]
    gain_list = [gain_own]
    refresh_list = [refreshed]
    total_sq = lax.psum(square_sum, ("shard", "tensor", "section"))
    entry_count = float(lax.axis_size("section") * layer_count * (D * FF + D))
    clip = jnp.minimum(1.0, lax.rsqrt(total_sq / entry_count + clip_eps))
    layer_index = 0
    first_new, second_new, direction = adam_direction(
        clip * proj_list[layer_index], first_moment[layer_index], second_moment[layer_index]
    )
    firsts = [first_new]
    seconds = [second_new]
    kept_basis = kept_list[layer_index]

    def fold_rows(total, piece, start, kept_basis=kept_basis):
        return jnp.dot(kept_basis, piece, precision=exact_mode)

    empty = jnp.zeros((rows_here, cols_here), jnp.float32)
    update_here = fold_rows(
        empty, lax.all_gather(direction, "shard", axis=0, tiled=True), jnp.int32(0)
    )
    updates = [update_here]
    refreshed = refresh_list[layer_index]
    frob = lax.psum(jnp.sum(refreshed * refreshed), ("shard", "tensor"))
    current = refreshed / jnp.sqrt(frob + ns_eps)
    gram = gram_of(current)
    for step_index in range(NS_STEPS):
        current = ns_update(current, gram)
        if step_index + 1 < NS_STEPS:
            gram = gram_of(current)
    bases = [current]
    gain_first_new, gain_second_new, gain_dir = adam_direction(
        clip * gain_list[layer_index], gain_first[layer_index], gain_second[layer_index]
    )
    gain_steps = [gain_dir]
    gain_firsts = [gain_first_new]
    gain_seconds = [gain_second_new]
    return (
        jnp.stack(updates),
        jnp.stack(firsts),
        jnp.stack(seconds),
        jnp.stack(bases),
        jnp.stack(gain_steps),
        jnp.stack(gain_firsts),
        jnp.stack(gain_seconds),
    )


def solution(mesh):
    placed = (
        P("section", "shard", None),
        P("section", "shard", "tensor"),
        P("section", "shard", None),
        P("section", "shard", "tensor"),
        P("section", "shard", "tensor"),
        P("section", "shard", None),
        P("section", "shard"),
        P("section", "shard"),
    )
    return jax.shard_map(
        shards,
        mesh=mesh,
        in_specs=placed,
        out_specs=(
            P("section", "shard", "tensor"),
            P("section", "shard", "tensor"),
            P("section", "shard", "tensor"),
            P("section", ("shard", "tensor"), None),
            P("section", "shard"),
            P("section", "shard"),
            P("section", "shard"),
        ),
        check_vma=False,
    )
```

profile of v0, /device:TPU:1, one launch (start us, length us, event | category | flops | bytes accessed | tf_op | source)
XLA Modules:
  0.0 854.7 jit_solution(13370359571268590590)
XLA Ops:
  7.2 24.3 %fusion = f32[2048,2048]{1,0:T(8,128)} fusion(bf16[1,2048,2048]{2,1,0:T(8,128)(2,1)} %param.9, bf16[1,2048,2048]{2,1,0:T(8,128)(2,1)} %param.8), kind=kOutput, calls=%fused_computation | convolution fusion | flops 17179869184 | bytes 33554432 | tf_op jit(solution)/shard_map/dot_general | solution.py:57
  31.6 94.5 %reduce-scatter.3.cloned.1.call-done = f32[256,2048]{1,0:T(8,128)} async-done(((f32[2048,2048]{1,0:T(8,128)}), f32[256,2048]{1,0:T(8,128)}) %reduce-scatter.3.cloned.1.call-update) | async-done | bytes 2097168 | tf_op jit(solution)/shard_map/reduce_scatter | solution.py:61
  126.1 6.4 convolution_bitcast_fusion.1
  132.6 64.0 %all-reduce.7.cloned.1.call-done = f32[256,2048]{0,1:T(8,128)} async-done(((f32[256,2048]{0,1:T(8,128)}), f32[256,2048]{0,1:T(8,128)}) %all-reduce.7.cloned.1.call-update) | async-done | bytes 2097168 | tf_op jit(solution)/shard_map/psum | solution.py:68
  196.6 4.2 fusion.17
  200.9 20.4 %reduce-scatter.5.cloned.1.call-done = f32[64,256]{1,0:T(8,128)} async-done(((f32[256,256]{1,0:T(8,128)}), f32[64,256]{1,0:T(8,128)}) %reduce-scatter.5.cloned.1.call-update) | async-done | bytes 65552 | tf_op jit(solution)/shard_map/reduce_scatter | solution.py:77
  221.2 1.5 multiply_reduce_fusion.1
  222.7 62.0 %psum.66 = f32[]{:T(128)} all-reduce(f32[]{:T(128)} %multiply_reduce_fusion.1), channel_id=1, replica_groups=mesh['shard'=8,'tensor'=4,'section'=4] {'shard','tensor'}, use_global_device_ids=true, to_apply=%region_8.0 | all-reduce | flops 1 | bytes 8 | tf_op jit(solution)/shard_map/psum | solution.py:109
  285.4 2.0 fusion.14
  287.5 104.3 %all-reduce.9.cloned.1.call-done = f32[256,256]{1,0:T(8,128)} async-done(((f32[256,256]{1,0:T(8,128)}), f32[256,256]{1,0:T(8,128)}) %all-reduce.9.cloned.1.call-update) | async-done | bytes 262160 | tf_op jit(solution)/shard_map/psum | solution.py:39
  391.8 1.5 fusion.7
  393.3 1.2 convolution_add_fusion.4
  395.8 101.9 %all-reduce.11.cloned.1.call-done = f32[256,256]{1,0:T(8,128)} async-done(((f32[256,256]{1,0:T(8,128)}), f32[256,256]{1,0:T(8,128)}) %all-reduce.11.cloned.1.call-update) | async-done | bytes 262160 | tf_op jit(solution)/shard_map/psum | solution.py:39
  497.7 1.5 fusion.6
  499.4 1.1 fusion.19
  500.7 1.3 copy.20
  501.9 2.3 copy.21
  504.2 13.5 %psum.63 = f32[2048]{0:T(1024)S(1)} all-reduce(f32[2048]{0:T(1024)S(1)} %bitcast.72), channel_id=1, replica_groups=mesh['shard'=8,'tensor'=4,'section'=4] {'shard'}, use_global_device_ids=true, to_apply=%region_2.0 | all-reduce | flops 2048 | bytes 16384 | tf_op jit(solution)/shard_map/psum | solution.py:68
  519.0 84.3 %all-reduce.13.cloned.1.call-done = f32[256,256]{1,0:T(8,128)} async-done(((f32[256,256]{1,0:T(8,128)}), f32[256,256]{1,0:T(8,128)}) %all-reduce.13.cloned.1.call-update) | async-done | bytes 262160 | tf_op jit(solution)/shard_map/psum | solution.py:39
  603.3 1.5 fusion.5
  606.3 1.1 multiply_reduce_fusion
  608.2 65.9 %psum.64 = f32[]{:T(128)} all-reduce(f32[]{:T(128)S(6)} %add.92), channel_id=1, replica_groups=mesh['shard'=8,'tensor'=4,'section'=4] {'shard','tensor','section'}, use_global_device_ids=true, to_apply=%region_4.0 | all-reduce | flops 1 | bytes 8 | tf_op jit(solution)/shard_map/psum | solution.py:89
  674.7 34.5 %all-reduce.15.cloned.1.call-done = f32[256,256]{1,0:T(8,128)} async-done(((f32[256,256]{1,0:T(8,128)}), f32[256,256]{1,0:T(8,128)}) %all-reduce.15.cloned.1.call-update) | async-done | bytes 262160 | tf_op jit(solution)/shard_map/psum | solution.py:39
  709.2 1.5 fusion.4
  711.0 1.1 fusion.21
  712.2 3.3 fusion.13
  715.5 2.3 copy.22
  720.6 93.8 %all-reduce.17.cloned.1.call-done = f32[256,256]{1,0:T(8,128)} async-done(((f32[256,256]{1,0:T(8,128)}), f32[256,256]{1,0:T(8,128)}) %all-reduce.17.cloned.1.call-update) | async-done | bytes 262160 | tf_op jit(solution)/shard_map/psum | solution.py:39
  814.4 1.5 fusion.3
  816.9 24.5 %all-gather.2.cloned.1.call-done = f32[256,2048]{1,0:T(8,128)} async-done(((f32[32,2048]{1,0:T(8,128)}), f32[256,2048]{1,0:T(8,128)}) %all-gather.2.cloned.1.call-update) | async-done | bytes 2097168 | tf_op jit(solution)/shard_map/all_gather | solution.py:105
  841.4 5.0 convolution_bitcast_fusion
  846.4 1.8 copy.23
  (44 shorter events, 8.0 us)
Async XLA Ops:
  7.2 119.0 %copy-start = (f32[1,256,256]{2,1,0:T(8,128)S(1)}, f32[1,256,256]{2,1,0:T(8,128)}, u32[]{:S(2)}) copy-start(f32[1,256,256]{2,1,0:T(8,128)} %param.10) | copy-start | bytes 786436
  7.2 119.0 %reduce-scatter.3.cloned.1.call-start = ((), (), s32[]{:S(2)}) async-start(), calls=%async_computation.2 | async-start | bytes 18874368 | tf_op jit(solution)/shard_map/reduce_scatter | solution.py:61
  31.5 165.1 %all-reduce.7.cloned.1.call-start = ((), (), s32[]{:S(2)}) async-start(), calls=%async_computation.3 | async-start | bytes 4194304 | tf_op jit(solution)/shard_map/psum | solution.py:68
  132.5 64.1 %copy-start.1 = (f32[256,2048]{1,0:T(8,128)S(1)}, f32[256,2048]{1,0:T(8,128)}, u32[]{:S(2)}) copy-start(f32[256,2048]{1,0:T(8,128)} %reduce-scatter.3.cloned.1.call-done) | copy-start | bytes 6291460
  132.5 88.7 %reduce-scatter.5.cloned.1.call-start = ((), (), s32[]{:S(2)}) async-start(), calls=%async_computation.5 | async-start | bytes 327680 | tf_op jit(solution)/shard_map/reduce_scatter | solution.py:77
  200.8 191.0 %all-reduce.9.cloned.1.call-start = ((), (), s32[]{:S(2)}) async-start(), calls=%async_computation.6 | async-start | bytes 524288 | tf_op jit(solution)/shard_map/psum | solution.py:39
  287.4 210.3 %all-reduce.11.cloned.1.call-start = ((), (), s32[]{:S(2)}) async-start(), calls=%async_computation.7 | async-start | bytes 524288 | tf_op jit(solution)/shard_map/psum | solution.py:39
  395.6 108.6 %copy-start.4 = (f32[1,1,2048]{2,1,0:T(1,128)S(1)}, f32[1,1,2048]{2,1,0:T(1,128)}, u32[]{:S(2)}) copy-start(f32[1,1,2048]{2,1,0:T(1,128)} %param.13) | copy-start | bytes 24580
  395.6 207.8 %all-reduce.13.cloned.1.call-start = ((), (), s32[]{:S(2)}) async-start(), calls=%async_computation.8 | async-start | bytes 524288 | tf_op jit(solution)/shard_map/psum | solution.py:39
  500.6 208.6 %all-reduce.15.cloned.1.call-start = ((), (), s32[]{:S(2)}) async-start(), calls=%async_computation.9 | async-start | bytes 524288 | tf_op jit(solution)/shard_map/psum | solution.py:39
  606.2 208.2 %all-reduce.17.cloned.1.call-start = ((), (), s32[]{:S(2)}) async-start(), calls=%async_computation.10 | async-start | bytes 524288 | tf_op jit(solution)/shard_map/psum | solution.py:39
  607.4 104.8 %copy-start.2 = (f32[1,32,2048]{1,2,0:T(8,128)S(1)}, f32[1,32,2048]{1,2,0:T(8,128)}, u32[]{:S(2)}) copy-start(f32[1,32,2048]{1,2,0:T(8,128)} %copy.21) | copy-start | bytes 786436
  712.1 5.7 copy-start.5
  712.1 5.8 copy-start.6
  712.1 129.2 %all-gather.2.cloned.1.call-start = ((), (), s32[]{:S(2)}) async-start(), calls=%async_computation.4 | async-start | bytes 2359296 | tf_op jit(solution)/shard_map/all_gather | solution.py:105
  715.5 3.1 copy-start.3
Sparse Core Ops, SparseCore 0:
  31.7 94.4 reduce-scatter.2
  132.6 63.9 all-reduce.6
  200.9 20.2 reduce-scatter.4
  287.6 104.1 all-reduce.8
  395.7 101.9 all-reduce.10
  501.4 101.9 all-reduce.12
  607.1 102.0 all-reduce.14
  712.4 101.9 all-reduce.16
  816.2 25.1 all-gather.1
where the time goes:
time: 855 us
  waiting for transfers between devices  622 us (73%)
  blocking collectives  141 us (16%)
  matrix products  56.7 us (7%)
  between operations  16.8 us (2%)
  local copies, waits for them, and re-layouts  9.74 us (1%)
    psum x5, waiting for transfers between devices, gram_of(): return lax.psum(local_gram, ('shard', 'tensor'))  419 us
    reduce_scatter x1, waiting for transfers between devices, shards(): lax.psum_scatter(row_term(jnp.int32(0), lax.axis_size('shard') * rows_her...  94.5 us
    psum x1, blocking collectives, shards(): total_sq = lax.psum(square_sum, ('shard', 'tensor', 'section'))  65.9 us
    psum x1, waiting for transfers between devices, shards(): lax.psum((part_proj, gain_partial[layer_index, 0]), 'shard')  64 us
    psum x1, blocking collectives, shards(): frob = lax.psum(jnp.sum(refreshed * refreshed), ('shard', 'tensor'))  62 us
    all_gather x1, waiting for transfers between devices, shards(): lax.all_gather(direction, 'shard', axis=0, tiled=True)  24.5 us
    dot_general x1, matrix products, row_term(): lax.dot_general(tokens_in, grads_out, (((0,), (0,)), ((), ())), preferred...  24.3 us
    reduce_scatter x1, waiting for transfers between devices, shards(): lax.psum_scatter(refresh_term(jnp.int32(0), lax.axis_size('tensor') * (ro...  20.4 us
  transfers between devices with their start and end apart: 9, of which 9 were waited for; matrix products, arithmetic and copies ran while one was open for 2% of the time, Pallas kernels for 0%

commit v1 on v0

--- a/solution.py
+++ b/solution.py
@@ -18,6 +18,11 @@
 coef_third = 2.0315
 
 
+def draw_the_scenes(m):
+    f_next = jnp.sum(lax.all_gather(m, ("shard", "tensor")), axis=0)
+    return f_next
+
+
 def adam_direction(clipped, first_old, second_old):
     first_new = beta_one * first_old + (1.0 - beta_one) * clipped
     second_new = beta_two * second_old + (1.0 - beta_two) * clipped * clipped
@@ -36,7 +41,7 @@
 
 def gram_of(block):
     local_gram = jnp.dot(block.T, block, precision=exact_mode)
-    return lax.psum(local_gram, ("shard", "tensor"))
+    return draw_the_scenes(local_gram)
 
 
 def shards(

time: 855 us -> 648 us (0.76)
  waiting for transfers between devices: 622 us -> 402 us
  other arithmetic: 7.26 us -> 26.9 us
    psum x5 -> x0, waiting for transfers between devices: 419 us -> none  [gram_of(): return lax.psum(local_gram, ('shard', 'tensor'))]
    all_gather x0 -> x5, waiting for transfers between devices: none -> 209 us  [draw_the_scenes(): f_next = jnp.sum(lax.all_gather(m, ('shard', 'tensor')), axis=0)]
    reduce_sum x0 -> x5, other arithmetic: none -> 19.7 us  [draw_the_scenes(): f_next = jnp.sum(lax.all_gather(m, ('shard', 'tensor')), axis=0)]
    all_gather x1, waiting for transfers between devices: 24.5 us -> 14.4 us  [shards(): lax.all_gather(direction, 'shard', axis=0, tiled=True)]
  transfers between devices with their start and end apart: 9 -> 9, of which waited for: 9 -> 8; matrix products, arithmetic and copies ran while one was open for 2% -> 4% of each run, Pallas kernels for 0% -> 0%
where the time goes in v1:
time: 648 us; the launch traced here: 647 us
  waiting for transfers between devices  402 us (62%)
  blocking collectives  141 us (22%)
  matrix products  50.2 us (8%)
  other arithmetic  26.9 us (4%)
  between operations  16.7 us (3%)
  local copies, waits for them, and re-layouts  9.67 us (1%)
    all_gather x5, waiting for transfers between devices, draw_the_scenes(): f_next = jnp.sum(lax.all_gather(m, ('shard', 'tensor')), axis=0)  209 us
    reduce_scatter x1, waiting for transfers between devices, shards(): lax.psum_scatter(row_term(jnp.int32(0), lax.axis_size('shard') * rows_her...  94.5 us
    psum x1, blocking collectives, shards(): total_sq = lax.psum(square_sum, ('shard', 'tensor', 'section'))  66.8 us
    psum x1, waiting for transfers between devices, shards(): lax.psum((part_proj, gain_partial[layer_index, 0]), 'shard')  64 us
    psum x1, blocking collectives, shards(): frob = lax.psum(jnp.sum(refreshed * refreshed), ('shard', 'tensor'))  62 us
    dot_general x1, matrix products, row_term(): lax.dot_general(tokens_in, grads_out, (((0,), (0,)), ((), ())), preferred...  24.3 us
    reduce_scatter x1, waiting for transfers between devices, shards(): lax.psum_scatter(refresh_term(jnp.int32(0), lax.axis_size('tensor') * (ro...  20.4 us
    reduce_sum x5, other arithmetic, draw_the_scenes(): f_next = jnp.sum(lax.all_gather(m, ('shard', 'tensor')), axis=0)  19.7 us
  transfers between devices with their start and end apart: 9, of which 8 were waited for; matrix products, arithmetic and copies ran while one was open for 4% of the time, Pallas kernels for 0%

profile of v1, /device:TPU:1, one launch (start us, length us, event | category | flops | bytes accessed | tf_op | source)
XLA Modules:
  0.0 647.4 jit_solution(5654392718103664544)
XLA Ops:
  7.2 24.3 %fusion = f32[2048,2048]{1,0:T(8,128)} fusion(bf16[1,2048,2048]{2,1,0:T(8,128)(2,1)} %param.9, bf16[1,2048,2048]{2,1,0:T(8,128)(2,1)} %param.8), kind=kOutput, calls=%fused_computation | convolution fusion | flops 17179869184 | bytes 33554432 | tf_op jit(solution)/shard_map/dot_general | solution.py:62
  31.6 94.5 %reduce-scatter.3.cloned.1.call-done = f32[256,2048]{1,0:T(8,128)} async-done(((f32[2048,2048]{1,0:T(8,128)}), f32[256,2048]{1,0:T(8,128)}) %reduce-scatter.3.cloned.1.call-update) | async-done | bytes 2097168 | tf_op jit(solution)/shard_map/reduce_scatter | solution.py:66
  126.1 6.4 convolution_bitcast_fusion.1
  132.6 64.0 %all-reduce.2.cloned.1.call-done = f32[256,2048]{0,1:T(8,128)} async-done(((f32[256,2048]{0,1:T(8,128)}), f32[256,2048]{0,1:T(8,128)}) %all-reduce.2.cloned.1.call-update) | async-done | bytes 2097168 | tf_op jit(solution)/shard_map/psum | solution.py:73
  196.6 4.2 fusion.17
  200.9 20.4 %reduce-scatter.5.cloned.1.call-done = f32[64,256]{1,0:T(8,128)} async-done(((f32[256,256]{1,0:T(8,128)}), f32[64,256]{1,0:T(8,128)}) %reduce-scatter.5.cloned.1.call-update) | async-done | bytes 65552 | tf_op jit(solution)/shard_map/reduce_scatter | solution.py:82
  221.2 1.5 multiply_reduce_fusion.1
  222.7 62.0 %psum.31 = f32[]{:T(128)} all-reduce(f32[]{:T(128)} %multiply_reduce_fusion.1), channel_id=1, replica_groups=mesh['shard'=8,'tensor'=4,'section'=4] {'shard','tensor'}, use_global_device_ids=true, to_apply=%region_8.0 | all-reduce | flops 1 | bytes 8 | tf_op jit(solution)/shard_map/psum | solution.py:114
  285.4 2.0 fusion.14
  287.5 55.1 %all-gather.14.cloned.1.call-done = f32[8192,256]{1,0:T(8,128)} async-done(((f32[256,256]{1,0:T(8,128)}), f32[8192,256]{1,0:T(8,128)}) %all-gather.14.cloned.1.call-update) | async-done | bytes 8388624 | tf_op jit(solution)/shard_map/all_gather | solution.py:22
  342.6 4.0 reduce_sum.75
  347.2 1.1 fusion.18
  348.5 52.3 %all-gather.16.cloned.1.call-done = f32[8192,256]{1,0:T(8,128)} async-done(((f32[256,256]{1,0:T(8,128)}), f32[8192,256]{1,0:T(8,128)}) %all-gather.16.cloned.1.call-update) | async-done | bytes 8388624 | tf_op jit(solution)/shard_map/all_gather | solution.py:22
  400.8 3.9 reduce_sum.76
  405.4 1.1 fusion.19
  406.6 52.5 %all-gather.18.cloned.1.call-done = f32[8192,256]{1,0:T(8,128)} async-done(((f32[256,256]{1,0:T(8,128)}), f32[8192,256]{1,0:T(8,128)}) %all-gather.18.cloned.1.call-update) | async-done | bytes 8388624 | tf_op jit(solution)/shard_map/all_gather | solution.py:22
  459.1 3.9 reduce_sum.77
  463.7 1.1 fusion.20
  464.9 1.3 copy.20
  466.2 2.3 copy.21
  468.4 12.3 %psum.28 = f32[2048]{0:T(1024)S(1)} all-reduce(f32[2048]{0:T(1024)S(1)} %bitcast.82), channel_id=1, replica_groups=mesh['shard'=8,'tensor'=4,'section'=4] {'shard'}, use_global_device_ids=true, to_apply=%region_2.0 | all-reduce | flops 2048 | bytes 16384 | tf_op jit(solution)/shard_map/psum | solution.py:73
  482.1 1.1 multiply_reduce_fusion
  483.8 66.8 %psum.29 = f32[]{:T(128)} all-reduce(f32[]{:T(128)S(6)} %add.82), channel_id=1, replica_groups=mesh['shard'=8,'tensor'=4,'section'=4] {'shard','tensor','section'}, use_global_device_ids=true, to_apply=%region_4.0 | all-reduce | flops 1 | bytes 8 | tf_op jit(solution)/shard_map/psum | solution.py:94
  551.4 3.3 fusion.13
  554.7 2.3 copy.22
  557.3 3.9 reduce_sum.78
  561.9 1.1 fusion.21
  565.7 14.4 %all-gather.12.cloned.1.call-done = f32[256,2048]{1,0:T(8,128)} async-done(((f32[32,2048]{1,0:T(8,128)}), f32[256,2048]{1,0:T(8,128)}) %all-gather.12.cloned.1.call-update) | async-done | bytes 2097168 | tf_op jit(solution)/shard_map/all_gather | solution.py:110
  580.1 5.0 convolution_bitcast_fusion
  585.1 1.8 copy.23
  587.0 48.7 %all-gather.22.cloned.1.call-done = f32[8192,256]{1,0:T(8,128)} async-done(((f32[256,256]{1,0:T(8,128)}), f32[8192,256]{1,0:T(8,128)}) %all-gather.22.cloned.1.call-update) | async-done | bytes 8388624 | tf_op jit(solution)/shard_map/all_gather | solution.py:22
  635.7 3.9 reduce_sum.79
  (47 shorter events, 8.1 us)
Async XLA Ops:
  7.2 119.0 %copy-start = (f32[1,256,256]{2,1,0:T(8,128)S(1)}, f32[1,256,256]{2,1,0:T(8,128)}, u32[]{:S(2)}) copy-start(f32[1,256,256]{2,1,0:T(8,128)} %param.10) | copy-start | bytes 786436
  7.2 119.0 %reduce-scatter.3.cloned.1.call-start = ((), (), s32[]{:S(2)}) async-start(), calls=%async_computation.2 | async-start | bytes 18874368 | tf_op jit(solution)/shard_map/reduce_scatter | solution.py:66
  31.5 165.1 %all-reduce.2.cloned.1.call-start = ((), (), s32[]{:S(2)}) async-start(), calls=%async_computation.3 | async-start | bytes 4194304 | tf_op jit(solution)/shard_map/psum | solution.py:73
  132.5 64.1 %copy-start.1 = (f32[256,2048]{1,0:T(8,128)S(1)}, f32[256,2048]{1,0:T(8,128)}, u32[]{:S(2)}) copy-start(f32[256,2048]{1,0:T(8,128)} %reduce-scatter.3.cloned.1.call-done) | copy-start | bytes 6291460
  132.5 88.7 %reduce-scatter.5.cloned.1.call-start = ((), (), s32[]{:S(2)}) async-start(), calls=%async_computation.5 | async-start | bytes 327680 | tf_op jit(solution)/shard_map/reduce_scatter | solution.py:82
  200.8 141.7 %all-gather.14.cloned.1.call-start = ((), (), s32[]{:S(2)}) async-start(), calls=%async_computation.6 | async-start | bytes 8650752 | tf_op jit(solution)/shard_map/all_gather | solution.py:22
  287.4 113.4 %all-gather.16.cloned.1.call-start = ((), (), s32[]{:S(2)}) async-start(), calls=%async_computation.7 | async-start | bytes 8650752 | tf_op jit(solution)/shard_map/all_gather | solution.py:22
  342.6 4.4 copy-start.2
  348.3 110.8 %all-gather.18.cloned.1.call-start = ((), (), s32[]{:S(2)}) async-start(), calls=%async_computation.8 | async-start | bytes 8650752 | tf_op jit(solution)/shard_map/all_gather | solution.py:22
  406.6 150.7 %all-gather.20.cloned.1.call-start = ((), (), s32[]{:S(2)}) async-start(), calls=%async_computation.9 | async-start | bytes 8650752 | tf_op jit(solution)/shard_map/all_gather | solution.py:22
  463.0 5.4 copy-start.3
  464.8 115.3 %all-gather.12.cloned.1.call-start = ((), (), s32[]{:S(2)}) async-start(), calls=%async_computation.4 | async-start | bytes 2359296 | tf_op jit(solution)/shard_map/all_gather | solution.py:110
  557.0 78.7 %all-gather.22.cloned.1.call-start = ((), (), s32[]{:S(2)}) async-start(), calls=%async_computation.10 | async-start | bytes 8650752 | tf_op jit(solution)/shard_map/all_gather | solution.py:22
  557.3 5.8 copy-start.4
  557.3 5.8 copy-start.5
Sparse Core Ops, SparseCore 0:
  31.7 94.4 reduce-scatter.2
  132.6 63.9 all-reduce.1
  200.9 20.2 reduce-scatter.4
  287.6 54.9 all-gather.13
  348.4 52.3 all-gather.15
  406.7 52.3 all-gather.17
  464.9 52.9 all-gather.19
  557.1 22.9 all-gather.11
  582.4 53.2 all-gather.21
